TPU v7x, 512 devices: a whole 4x4x16 slice. The times are simulated.
512 devices in a mesh: seq: 64 (over x, z), head: 8 (over y, core).
Axes of the slice: x: 4, y: 4, z: 16, core: 2. Of those that a mesh axis runs over, the one named last changes fastest.
Arguments:
- tokens: bfloat16 [16384, 4096], P('seq', 'head'), may hold values from -40 to 40
- queries: bfloat16 [16384, 4096], P('seq', 'head'), may hold values from -6 to 6
- key_rows: bfloat16 [16384, 4096], P('seq', 'head'), may hold values from -6 to 6
- values: bfloat16 [16384, 4096], P('seq', 'head'), may hold values from -6 to 6
- log_decay: float32 [32, 16384], P('head', 'seq'), may hold values from -1 to 0
- head_gain: float32 [4096], P('head'), may hold values from 0.5 to 1.5
- expert_gain: float32 [4096], P('head'), may hold values from 0.5 to 1.5
- route_ids: int32 [16384, 2], P('seq'), may hold values from 0 to 31, all different within a row; in each aligned block of 256 rows (0 to 255, 256 to 511, ...) at most 20 rows name the same one
- route_weight: float32 [16384, 2], P('seq'), may hold values from 0.2 to 1
- expert_in: bfloat16 [64, 4096, 1408], P('seq', 'head'), may hold values from -0.09375 to 0.09375
- expert_out: bfloat16 [64, 704, 4096], P('seq', None, 'head'), may hold values from -0.15625 to 0.15625
Outputs:
- mixed: bfloat16 [16384, 4096], P('seq', 'head')
Inputs may be any that keep to these rules, and one draw needn't show every extreme that they name: `route_ids`: within the rows of one device (aligned blocks of 256 tokens) no expert is named by more than 20 tokens, a bound that some block reaches; a token's two experts differ.
All inputs are finite; a program needn't handle non-finite values.
Results may differ from a plain program's by a relative error of at most 0.015.
Values may be sent and summed in bfloat16 or wider, within the bound.
No kernel may reach another device: no remote copies, remote signals or barrier semaphores. Data moves between devices by JAX's collectives and lax.ppermute only.
A program may use at most 64 MiB of HBM per device.

v0:
```python
import jax
import jax.numpy as jnp
from jax import lax
from jax.sharding import PartitionSpec as P

D = 4096
EXPERTS = 32
CAP = 20
CHUNKS = ((0, 10), (10, 20))
EPSILON = 1e-06


def exclusive_scan(decay, state, axis):
    place = lax.axis_index(axis)
    count = lax.axis_size(axis)
    heads, rows, cols = state.shape
    own = jnp.concatenate([state, jnp.broadcast_to(decay[:, None, None], (heads, 1, cols))], axis=1)
    window = own
    before_decay = jnp.ones_like(decay)
    before_state = jnp.zeros_like(state)
    shift = 1
    while shift < count:
        pairs = [(j, j + shift) for j in range(count - shift)]
        got = lax.ppermute(window, axis, pairs)
        valid = place >= shift
        got_state = got[:, :rows, :]
        got_decay = jnp.where(valid, got[:, rows, 0], 1.0)
        before_state = before_decay[:, None, None] * got_state + before_state
        before_decay = before_decay * got_decay
        window_decay = window[:, rows, 0]
        window_state = window_decay[:, None, None] * got_state + window[:, :rows, :]
        window_decay = window_decay * got_decay
        window = jnp.concatenate(
            [window_state, jnp.broadcast_to(window_decay[:, None, None], (heads, 1, cols))], axis=1
        )
        shift *= 2
    return before_state


def per_device(
    tokens,
    queries,
    key_rows,
    values,
    log_decay,
    head_gain,
    expert_gain,
    route_ids,
    route_weight,
    expert_in,
    expert_out,
):
    length = tokens.shape[0]
    local_width = tokens.shape[1]
    heads_here = log_decay.shape[0]
    head_size = queries.shape[1] // heads_here
    score_scale = head_size ** (-0.5)
    query_heads = queries.reshape(length, heads_here, head_size)
    key_heads = key_rows.reshape(length, heads_here, head_size)
    value_heads = values.reshape(length, heads_here, head_size)
    cumulative = jnp.cumsum(log_decay, axis=1)
    causal = (jnp.arange(length)[:, None] >= jnp.arange(length)[None, :])[None]
    scores = (
        jnp.einsum("thd,shd->hts", query_heads, key_heads, preferred_element_type=jnp.float32)
        * score_scale
    )
    spread = cumulative[:, :, None] - cumulative[:, None, :]
    mixing = jnp.where(causal, scores * jnp.exp(jnp.where(causal, spread, 0.0)), 0.0).astype(
        jnp.bfloat16
    )
    inside = jnp.einsum("hts,shd->thd", mixing, value_heads, preferred_element_type=jnp.float32)
    to_end = jnp.exp(cumulative[:, -1:] - cumulative)
    carried_keys = (key_heads.astype(jnp.float32) * to_end.T[:, :, None]).astype(jnp.bfloat16)
    block_state = jnp.einsum(
        "shd,she->hde", carried_keys, value_heads, preferred_element_type=jnp.float32
    )
    block_decay = jnp.exp(cumulative[:, -1])
    entering = exclusive_scan(block_decay, block_state, "seq")
    from_before = jnp.einsum(
        "thd,hde->the",
        query_heads.astype(jnp.float32),
        entering,
        precision=lax.Precision.HIGHEST,
        preferred_element_type=jnp.float32,
    )
    attended = inside + from_before * (jnp.exp(cumulative).T[:, :, None] * score_scale)
    head_rms = lax.rsqrt(jnp.mean(attended * attended, axis=2, keepdims=True) + EPSILON)
    normed_heads = (attended * head_rms).reshape(length, local_width)
    hidden_state = (tokens.astype(jnp.float32) + normed_heads * head_gain).astype(jnp.bfloat16)
    hidden_wide = hidden_state.astype(jnp.float32)
    local_squares = jnp.sum(hidden_wide * hidden_wide, axis=1)
    total_squares = lax.psum(local_squares, "head")
    inverse_rms = lax.rsqrt(total_squares / D + EPSILON)
    expert_input = (hidden_wide * inverse_rms[:, None] * expert_gain).astype(jnp.bfloat16)
    capacity = CAP
    expert_count = EXPERTS
    flat_ids = route_ids.reshape(-1)
    pair_count = flat_ids.shape[0]
    chosen = (flat_ids[:, None] == jnp.arange(expert_count)[None, :]).astype(jnp.float32)
    strictly_before = (jnp.arange(pair_count)[:, None] > jnp.arange(pair_count)[None, :]).astype(
        jnp.float32
    )
    earlier_counts = jnp.dot(
        strictly_before, chosen, precision=lax.Precision.HIGHEST, preferred_element_type=jnp.float32
    )
    slot_index = jnp.sum(earlier_counts * chosen, axis=1).astype(jnp.int32)
    position = (flat_ids * capacity + slot_index).reshape(length, route_ids.shape[1])
    slot_ids = jnp.arange(expert_count * capacity, dtype=jnp.int32)
    picks = position[None, :, :] == slot_ids[:, None, None]
    dispatch_matrix = jnp.any(picks, axis=2).astype(jnp.bfloat16)
    send_rows = jnp.dot(dispatch_matrix, expert_input, preferred_element_type=jnp.float32).astype(
        jnp.bfloat16
    )
    hidden_split = expert_in.shape[0] * lax.axis_size("seq") // expert_count
    send_buffer = jnp.repeat(
        send_rows.reshape(expert_count, 1, capacity, local_width), hidden_split, axis=0
    )
    block_units = expert_out.shape[1]
    pieces = []
    earlier = None
    for lo, hi in CHUNKS:
        arrived = lax.all_to_all(
            send_buffer[:, :, lo:hi], "seq", split_axis=0, concat_axis=1, tiled=True
        )
        blocks_here, sources, item_count, feature_count = arrived.shape
        flat_rows = arrived.reshape(blocks_here, sources * item_count, feature_count)
        partial_sums = jnp.einsum(
            "erd,edh->erh", flat_rows, expert_in, preferred_element_type=jnp.float32
        )
        partial_sums = partial_sums.reshape(blocks_here, sources, item_count, 2, block_units)
        if earlier is not None:
            partial_sums, earlier = lax.optimization_barrier((partial_sums, earlier))
        gate_up = lax.psum(partial_sums.astype(jnp.bfloat16), "head").astype(jnp.float32)
        earlier = gate_up
        activated = (jax.nn.silu(gate_up[:, :, :, 0]) * gate_up[:, :, :, 1]).astype(jnp.bfloat16)
        activated = activated.reshape(blocks_here, sources * item_count, block_units)
        produced = jnp.einsum(
            "erh,ehd->erd", activated, expert_out, preferred_element_type=jnp.float32
        ).astype(jnp.bfloat16)
        computed = produced.reshape(blocks_here, sources, item_count, feature_count)
        returned = lax.all_to_all(computed, "seq", split_axis=1, concat_axis=0, tiled=True)
        pieces.append(
            jnp.sum(
                returned.reshape(expert_count, hidden_split, item_count, local_width).astype(
                    jnp.float32
                ),
                axis=1,
            )
        )
    merged = jnp.concatenate(pieces, axis=1)
    merged = merged.reshape(expert_count * capacity, local_width)
    slot_rows = merged[position]
    expert_mix = jnp.sum(slot_rows * route_weight[:, :, None], axis=1)
    return (hidden_wide + expert_mix).astype(jnp.bfloat16)


def solution(mesh):
    return jax.shard_map(
        per_device,
        mesh=mesh,
        in_specs=(
            P("seq", "head"),
            P("seq", "head"),
            P("seq", "head"),
            P("seq", "head"),
            P("head", "seq"),
            P("head"),
            P("head"),
            P("seq", None),
            P("seq", None),
            P("seq", "head", None),
            P("seq", None, "head"),
        ),
        out_specs=P("seq", "head"),
        check_vma=False,
    )
```

profile of v0, /device:TPU:31, one launch (start us, length us, event | category | flops | bytes accessed | tf_op | source)
XLA Modules:
  0.0 501.7 jit_solution(16637249077426523019)
XLA Ops:
  11.5 3.5 collective-permute-start
  15.1 14.2 %collective-permute-done = f32[4,129,128]{2,1,0:T(8,128)S(1)} collective-permute-done((f32[4,129,128]{2,1,0:T(8,128)S(1)}, f32[4,129,128]{2,1,0:T(8,128)S(1)}, u32[]{:S(2)}, u32[]{:S(2)}) %collective-permute-start) | collective-permute-done | bytes 264224 | tf_op jit(solution)/shard_map/ppermute | solution.py:24
  29.6 1.9 collective-permute-start.1
  31.7 15.9 %collective-permute-done.1 = f32[4,129,128]{2,1,0:T(8,128)S(1)} collective-permute-done((f32[4,129,128]{2,1,0:T(8,128)S(1)}, f32[4,129,128]{2,1,0:T(8,128)S(1)}, u32[]{:S(2)}, u32[]{:S(2)}) %collective-permute-start.1) | collective-permute-done | bytes 264224 | tf_op jit(solution)/shard_map/ppermute | solution.py:24
  47.9 1.9 collective-permute-start.2
  49.8 27.7 %collective-permute-done.2 = f32[4,129,128]{2,1,0:T(8,128)S(1)} collective-permute-done((f32[4,129,128]{2,1,0:T(8,128)S(1)}, f32[4,129,128]{2,1,0:T(8,128)S(1)}, u32[]{:S(2)}, u32[]{:S(2)}) %collective-permute-start.2) | collective-permute-done | bytes 264224 | tf_op jit(solution)/shard_map/ppermute | solution.py:24
  77.8 1.9 collective-permute-start.3
  80.5 24.4 %collective-permute-done.3 = f32[4,129,128]{2,1,0:T(8,128)S(1)} collective-permute-done((f32[4,129,128]{2,1,0:T(8,128)S(1)}, f32[4,129,128]{2,1,0:T(8,128)S(1)}, u32[]{:S(2)}, u32[]{:S(2)}) %collective-permute-start.3) | collective-permute-done | bytes 264224 | tf_op jit(solution)/shard_map/ppermute | solution.py:24
  107.5 7.3 %collective-permute-done.4 = f32[4,129,128]{2,1,0:T(8,128)S(1)} collective-permute-done((f32[4,129,128]{2,1,0:T(8,128)S(1)}, f32[4,129,128]{2,1,0:T(8,128)S(1)}, u32[]{:S(2)}, u32[]{:S(2)}) %collective-permute-start.4) | collective-permute-done | bytes 264224 | tf_op jit(solution)/shard_map/ppermute | solution.py:24
  118.8 7.5 %collective-permute-done.5 = f32[4,129,128]{2,1,0:T(8,128)} collective-permute-done((f32[4,129,128]{2,1,0:T(8,128)}, f32[4,129,128]{2,1,0:T(8,128)}, u32[]{:S(2)}, u32[]{:S(2)}) %collective-permute-start.5) | collective-permute-done | bytes 264224 | tf_op jit(solution)/shard_map/ppermute | solution.py:24
  128.9 11.9 %psum.21 = f32[256]{0:T(256)S(1)} all-reduce(f32[256]{0:T(256)S(1)} %get-tuple-element.18), channel_id=1, replica_groups=mesh['seq'=64,'head'=8] {'head'}, use_global_device_ids=true, to_apply=%region_6.7 | all-reduce | flops 256 | bytes 2048 | tf_op jit(solution)/shard_map/psum | solution.py:92
  143.1 62.9 %all_to_all.16 = bf16[64,1,10,512]{3,2,1,0:T(8,128)(2,1)S(1)} all-to-all(bf16[64,1,10,512]{3,2,1,0:T(8,128)(2,1)S(1)} %get-tuple-element.22), channel_id=1, replica_groups=mesh['seq'=64,'head'=8] {'seq'}, dimensions={0} | all-to-all | bytes 1310720 | tf_op jit(solution)/shard_map/all_to_all | solution.py:122
  206.0 10.2 %all-to-all-start.2 = ((bf16[64,1,10,512]{3,2,1,0:T(8,128)(2,1)}), bf16[64,1,10,512]{3,2,1,0:T(8,128)(2,1)}, u32[]{:S(2)}, u32[]{:S(2)}) async-start(bf16[64,1,10,512]{3,2,1,0:T(8,128)(2,1)} %get-tuple-element.23), calls=%async_computation.2 | async-start | bytes 2097152 | tf_op jit(solution)/shard_map/all_to_all | solution.py:122
  217.9 4.0 convert_bitcast_fusion
  221.9 81.9 %all-reduce.3.cloned.1.call-done = bf16[1,64,10,2,704]{4,1,3,2,0:T(8,128)(2,1)} async-done(((bf16[1,64,10,2,704]{4,1,3,2,0:T(8,128)(2,1)}), bf16[1,64,10,2,704]{4,1,3,2,0:T(8,128)(2,1)}) %all-reduce.3.cloned.1.call-update) | async-done | bytes 1802256 | tf_op jit(solution)/shard_map/psum | solution.py:133
  303.8 2.0 convert_element_type.115
  309.5 15.4 %all-to-all-start.1 = ((bf16[1,64,10,512]{3,2,0,1:T(8,128)(2,1)}), bf16[1,64,10,512]{3,2,0,1:T(8,128)(2,1)S(1)}, u32[]{:S(2)}, u32[]{:S(2)}) async-start(bf16[1,64,10,512]{3,2,0,1:T(8,128)(2,1)} %bitcast.18), calls=%async_computation.1 | async-start | bytes 2097152 | tf_op jit(solution)/shard_map/all_to_all | solution.py:141
  324.9 3.8 convolution_bitcast_fusion
  328.8 80.3 %all-reduce.5.cloned.1.call-done = bf16[1,64,10,2,704]{4,1,3,2,0:T(8,128)(2,1)} async-done(((bf16[1,64,10,2,704]{4,1,3,2,0:T(8,128)(2,1)}), bf16[1,64,10,2,704]{4,1,3,2,0:T(8,128)(2,1)}) %all-reduce.5.cloned.1.call-update) | async-done | bytes 1802256 | tf_op jit(solution)/shard_map/psum | solution.py:133
  409.0 2.0 convert_element_type.122
  413.6 1.9 convolution_convert_fusion
  416.7 15.5 %all-to-all-start.3 = ((bf16[1,64,10,512]{3,2,0,1:T(8,128)(2,1)}), bf16[1,64,10,512]{3,2,0,1:T(8,128)(2,1)}, u32[]{:S(2)}, u32[]{:S(2)}) async-start(bf16[1,64,10,512]{3,2,0,1:T(8,128)(2,1)} %bitcast.27), calls=%async_computation.3 | async-start | bytes 2097152 | tf_op jit(solution)/shard_map/all_to_all | solution.py:141
  433.0 53.0 %all-to-all-done.3 = bf16[1,64,10,512]{3,2,0,1:T(8,128)(2,1)} async-done(((bf16[1,64,10,512]{3,2,0,1:T(8,128)(2,1)}), bf16[1,64,10,512]{3,2,0,1:T(8,128)(2,1)}, u32[]{:S(2)}, u32[]{:S(2)}) %all-to-all-start.3) | async-done | bytes 655392 | tf_op jit(solution)/shard_map/all_to_all | solution.py:141
  485.9 1.6 convert_reduce_fusion
  (116 shorter events, 35.1 us)
Async XLA Ops:
  6.5 301.0 %copy-start = (bf16[1,704,512]{2,1,0:T(8,128)(2,1)S(1)}, bf16[1,704,512]{2,1,0:T(8,128)(2,1)}, u32[]{:S(2)}) copy-start(bf16[1,704,512]{2,1,0:T(8,128)(2,1)} %param.21) | copy-start | bytes 2162692
  11.5 17.8 %collective-permute-start = (f32[4,129,128]{2,1,0:T(8,128)S(1)}, f32[4,129,128]{2,1,0:T(8,128)S(1)}, u32[]{:S(2)}, u32[]{:S(2)}) collective-permute-start(f32[4,129,128]{2,1,0:T(8,128)S(1)} %pad_maximum_fusion.1), channel_id=1, source_target_pairs={{0,8},{8,16},{16,24},{24,32},{32,40},{40,48},{48,56},{56,64},{64,7... | collective-permute-start | bytes 792584 | tf_op jit(solution)/shard_map/ppermute | solution.py:24
  29.4 50.3 %copy-start.8 = (s32[256,2]{0,1:T(2,128)S(1)}, s32[256,2]{0,1:T(2,128)}, u32[]{:S(2)}) copy-start(s32[256,2]{0,1:T(2,128)} %param.18) | copy-start | bytes 6148
  29.6 17.9 %collective-permute-start.1 = (f32[4,129,128]{2,1,0:T(8,128)S(1)}, f32[4,129,128]{2,1,0:T(8,128)S(1)}, u32[]{:S(2)}, u32[]{:S(2)}) collective-permute-start(f32[4,129,128]{2,1,0:T(8,128)S(1)} %pad_maximum_fusion.2), channel_id=1, source_target_pairs={{0,16},{8,24},{16,32},{24,40},{32,48},{40,56},{48,64},{56,72},{64,... | collective-permute-start | bytes 792584 | tf_op jit(solution)/shard_map/ppermute | solution.py:24
  47.9 29.6 %collective-permute-start.2 = (f32[4,129,128]{2,1,0:T(8,128)S(1)}, f32[4,129,128]{2,1,0:T(8,128)S(1)}, u32[]{:S(2)}, u32[]{:S(2)}) collective-permute-start(f32[4,129,128]{2,1,0:T(8,128)S(1)} %pad_maximum_fusion.3), channel_id=1, source_target_pairs={{0,32},{8,40},{16,48},{24,56},{32,64},{40,72},{48,80},{56,88},{64,... | collective-permute-start | bytes 792584 | tf_op jit(solution)/shard_map/ppermute | solution.py:24
  77.8 27.2 %collective-permute-start.3 = (f32[4,129,128]{2,1,0:T(8,128)S(1)}, f32[4,129,128]{2,1,0:T(8,128)S(1)}, u32[]{:S(2)}, u32[]{:S(2)}) collective-permute-start(f32[4,129,128]{2,1,0:T(8,128)S(1)} %pad_maximum_fusion.4), channel_id=1, source_target_pairs={{0,64},{8,72},{16,80},{24,88},{32,96},{40,104},{48,112},{56,120},{... | collective-permute-start | bytes 792584 | tf_op jit(solution)/shard_map/ppermute | solution.py:24
  105.3 9.5 %collective-permute-start.4 = (f32[4,129,128]{2,1,0:T(8,128)S(1)}, f32[4,129,128]{2,1,0:T(8,128)S(1)}, u32[]{:S(2)}, u32[]{:S(2)}) collective-permute-start(f32[4,129,128]{2,1,0:T(8,128)S(1)} %pad_maximum_fusion.5), channel_id=1, source_target_pairs={{0,128},{8,136},{16,144},{24,152},{32,160},{40,168},{48,176},{56,1... | collective-permute-start | bytes 792584 | tf_op jit(solution)/shard_map/ppermute | solution.py:24
  115.0 11.2 %copy-start.6 = (bf16[256,512]{1,0:T(8,128)(2,1)S(1)}, bf16[256,512]{1,0:T(8,128)(2,1)}, u32[]{:S(2)}) copy-start(bf16[256,512]{1,0:T(8,128)(2,1)} %param.12) | copy-start | bytes 786436
  115.8 10.4 %collective-permute-start.5 = (f32[4,129,128]{2,1,0:T(8,128)}, f32[4,129,128]{2,1,0:T(8,128)}, u32[]{:S(2)}, u32[]{:S(2)}) collective-permute-start(f32[4,129,128]{2,1,0:T(8,128)} %pad_maximum_fusion.6), channel_id=1, source_target_pairs={{0,256},{8,264},{16,272},{24,280},{32,288},{40,296},{48,304},{56,3... | collective-permute-start | bytes 792584 | tf_op jit(solution)/shard_map/ppermute | solution.py:24
  126.3 1.8 copy-start.9
  127.8 1.0 copy-start.5
  127.8 13.0 %copy-start.7 = (pred[640,256]{1,0:T(8,128)(4,1)S(1)}, pred[640,256]{1,0:T(8,128)(4,1)}, u32[]{:S(2)}) copy-start(pred[640,256]{1,0:T(8,128)(4,1)} %fusion.4) | copy-start | bytes 491524
  127.8 13.0 %copy-start.11 = (f32[512]{0:T(512)S(1)}, f32[512]{0:T(512)}, u32[]{:S(2)}) copy-start(f32[512]{0:T(512)} %param.17) | copy-start | bytes 6148
  128.9 11.9 %copy-start.3 = (bf16[256,512]{1,0:T(8,128)(2,1)}, bf16[256,512]{1,0:T(8,128)(2,1)S(1)}, u32[]{:S(2)}) copy-start(bf16[256,512]{1,0:T(8,128)(2,1)S(1)} %get-tuple-element.19) | copy-start | bytes 786436
  143.1 73.2 %copy-start.1 = (bf16[1,512,1408]{2,1,0:T(8,128)(2,1)S(1)}, bf16[1,512,1408]{2,1,0:T(8,128)(2,1)}, u32[]{:S(2)}) copy-start(bf16[1,512,1408]{2,1,0:T(8,128)(2,1)} %param.20) | copy-start | bytes 4325380
  206.0 103.5 %all-to-all-start.2 = ((bf16[64,1,10,512]{3,2,1,0:T(8,128)(2,1)}), bf16[64,1,10,512]{3,2,1,0:T(8,128)(2,1)}, u32[]{:S(2)}, u32[]{:S(2)}) async-start(bf16[64,1,10,512]{3,2,1,0:T(8,128)(2,1)} %get-tuple-element.23), calls=%async_computation.2 | async-start | bytes 2097152 | tf_op jit(solution)/shard_map/all_to_all | solution.py:122
  216.2 87.5 %all-reduce.3.cloned.1.call-start = ((), (), s32[]{:S(2)}) async-start(), calls=%async_computation.4 | async-start | bytes 3932160 | tf_op jit(solution)/shard_map/psum | solution.py:133
  308.3 16.7 %copy-start.2 = (bf16[1,512,1408]{1,2,0:T(8,128)(2,1)S(1)}, bf16[1,512,1408]{1,2,0:T(8,128)(2,1)}, u32[]{:S(2)}) copy-start(bf16[1,512,1408]{1,2,0:T(8,128)(2,1)} %copy.107) | copy-start | bytes 4325380
  309.5 107.2 %all-to-all-start.1 = ((bf16[1,64,10,512]{3,2,0,1:T(8,128)(2,1)}), bf16[1,64,10,512]{3,2,0,1:T(8,128)(2,1)S(1)}, u32[]{:S(2)}, u32[]{:S(2)}) async-start(bf16[1,64,10,512]{3,2,0,1:T(8,128)(2,1)} %bitcast.18), calls=%async_computation.1 | async-start | bytes 2097152 | tf_op jit(solution)/shard_map/all_to_all | solution.py:141
  324.9 84.2 %all-reduce.5.cloned.1.call-start = ((), (), s32[]{:S(2)}) async-start(), calls=%async_computation.5 | async-start | bytes 3932160 | tf_op jit(solution)/shard_map/psum | solution.py:133
  415.5 16.8 %copy-start.10 = (f32[256,2]{0,1:T(2,128)S(1)}, f32[256,2]{0,1:T(2,128)}, u32[]{:S(2)}) copy-start(f32[256,2]{0,1:T(2,128)} %param.19) | copy-start | bytes 6148
  416.7 69.2 %all-to-all-start.3 = ((bf16[1,64,10,512]{3,2,0,1:T(8,128)(2,1)}), bf16[1,64,10,512]{3,2,0,1:T(8,128)(2,1)}, u32[]{:S(2)}, u32[]{:S(2)}) async-start(bf16[1,64,10,512]{3,2,0,1:T(8,128)(2,1)} %bitcast.27), calls=%async_computation.3 | async-start | bytes 2097152 | tf_op jit(solution)/shard_map/all_to_all | solution.py:141
  492.0 2.0 copy-start.4
Sparse Core Ops, SparseCore 0:
  222.0 81.7 all-reduce.2
  328.9 80.1 all-reduce.4
where the time goes:
time: 503 us; the launch traced here: 502 us
  waiting for transfers between devices  312 us (62%)
  blocking collectives  74.8 us (15%)
  starting transfers between devices  53.1 us (11%)
  local copies, waits for them, and re-layouts  17.3 us (3%)
  matrix products  15.4 us (3%)
  other arithmetic  15 us (3%)
  between operations  14 us (3%)
    psum x2, waiting for transfers between devices, per_device(): lax.psum(partial_sums.astype(jnp.bfloat16), 'head').astype(jnp.float32)  162 us
    ppermute x6, waiting for transfers between devices, exclusive_scan(): got = lax.ppermute(window, axis, pairs)  97 us
    all_to_all x1, blocking collectives, per_device(): lax.all_to_all(send_buffer[:, :, lo:hi], 'seq', split_axis=0, concat_axis...  62.9 us
    all_to_all x2, waiting for transfers between devices, per_device(): lax.all_to_all(computed, 'seq', split_axis=1, concat_axis=0, tiled=True)  53 us
    all_to_all x2, starting transfers between devices, per_device(): lax.all_to_all(computed, 'seq', split_axis=1, concat_axis=0, tiled=True)  30.9 us
    ppermute x6, starting transfers between devices, exclusive_scan(): got = lax.ppermute(window, axis, pairs)  11.9 us
    psum x1, blocking collectives, per_device(): total_squares = lax.psum(local_squares, 'head')  11.9 us
    all_to_all x1, starting transfers between devices, per_device(): lax.all_to_all(send_buffer[:, :, lo:hi], 'seq', split_axis=0, concat_axis...  10.2 us
  transfers between devices with their start and end apart: 11, of which 9 were waited for; matrix products, arithmetic and copies ran while one was open for 5% of the time, Pallas kernels for 0%

commit v1 on v0

--- a/solution.py
+++ b/solution.py
@@ -1,3 +1,4 @@
+import functools
 import jax
 import jax.numpy as jnp
 from jax import lax
@@ -8,6 +9,19 @@
 CAP = 20
 CHUNKS = ((0, 10), (10, 20))
 EPSILON = 1e-06
+
+
+def _begin_indices(in_array, net_axis):
+    a_next = lax.all_to_all(
+        jnp.stack(jnp.split(in_array, lax.axis_size(net_axis), axis=0), axis=0),
+        net_axis,
+        split_axis=0,
+        concat_axis=0,
+    )
+    return jnp.concatenate(a_next, axis=1)
+
+
+loads_fit = functools.partial(_begin_indices, net_axis="seq")
 
 
 def exclusive_scan(decay, state, axis):
@@ -119,9 +133,7 @@
     pieces = []
     earlier = None
     for lo, hi in CHUNKS:
-        arrived = lax.all_to_all(
-            send_buffer[:, :, lo:hi], "seq", split_axis=0, concat_axis=1, tiled=True
-        )
+        arrived = loads_fit(send_buffer[:, :, lo:hi])
         blocks_here, sources, item_count, feature_count = arrived.shape
         flat_rows = arrived.reshape(blocks_here, sources * item_count, feature_count)
         partial_sums = jnp.einsum(

time: 503 us -> 540 us (1.074)
  local copies, waits for them, and re-layouts: 17.3 us -> 54.4 us
    unnamed x29 -> x91, local copies, waits for them, and re-layouts: 2.64 us -> 40.6 us
where the time goes in v1:
time: 540 us; the launch traced here: 539 us
  waiting for transfers between devices  312 us (58%)
  blocking collectives  74.8 us (14%)
  local copies, waits for them, and re-layouts  54.4 us (10%)
  starting transfers between devices  53.4 us (10%)
  matrix products  15.5 us (3%)
  other arithmetic  14.7 us (3%)
  between operations  14 us (3%)
    psum x2, waiting for transfers between devices, per_device(): lax.psum(partial_sums.astype(jnp.bfloat16), 'head').astype(jnp.float32)  162 us
    ppermute x6, waiting for transfers between devices, exclusive_scan(): got = lax.ppermute(window, axis, pairs)  96.8 us
    all_to_all x1, blocking collectives, _begin_indices(): lax.all_to_all(jnp.stack(jnp.split(in_array, lax.axis_size(net_axis), axi...  62.9 us
    all_to_all x2, waiting for transfers between devices, per_device(): lax.all_to_all(computed, 'seq', split_axis=1, concat_axis=0, tiled=True)  53 us
    unnamed x91, local copies, waits for them, and re-layouts  40.6 us
    all_to_all x2, starting transfers between devices, per_device(): lax.all_to_all(computed, 'seq', split_axis=1, concat_axis=0, tiled=True)  31.1 us
    ppermute x6, starting transfers between devices, exclusive_scan(): got = lax.ppermute(window, axis, pairs)  11.9 us
    psum x1, blocking collectives, per_device(): total_squares = lax.psum(local_squares, 'head')  11.9 us
  transfers between devices with their start and end apart: 11, of which 9 were waited for; matrix products, arithmetic and copies ran while one was open for 5% of the time, Pallas kernels for 0%

profile of v1, /device:TPU:31, one launch (start us, length us, event | category | flops | bytes accessed | tf_op | source)
XLA Modules:
  0.0 538.9 jit_solution(4526771121444809620)
XLA Ops:
  12.0 3.5 collective-permute-start
  15.6 14.2 %collective-permute-done = f32[4,129,128]{2,1,0:T(8,128)S(1)} collective-permute-done((f32[4,129,128]{2,1,0:T(8,128)S(1)}, f32[4,129,128]{2,1,0:T(8,128)S(1)}, u32[]{:S(2)}, u32[]{:S(2)}) %collective-permute-start) | collective-permute-done | bytes 264224 | tf_op jit(solution)/shard_map/ppermute | solution.py:38
  30.1 1.9 collective-permute-start.1
  32.1 16.0 %collective-permute-done.1 = f32[4,129,128]{2,1,0:T(8,128)S(1)} collective-permute-done((f32[4,129,128]{2,1,0:T(8,128)S(1)}, f32[4,129,128]{2,1,0:T(8,128)S(1)}, u32[]{:S(2)}, u32[]{:S(2)}) %collective-permute-start.1) | collective-permute-done | bytes 264224 | tf_op jit(solution)/shard_map/ppermute | solution.py:38
  48.4 1.9 collective-permute-start.2
  50.3 27.6 %collective-permute-done.2 = f32[4,129,128]{2,1,0:T(8,128)S(1)} collective-permute-done((f32[4,129,128]{2,1,0:T(8,128)S(1)}, f32[4,129,128]{2,1,0:T(8,128)S(1)}, u32[]{:S(2)}, u32[]{:S(2)}) %collective-permute-start.2) | collective-permute-done | bytes 264224 | tf_op jit(solution)/shard_map/ppermute | solution.py:38
  78.2 1.9 collective-permute-start.3
  81.0 24.5 %collective-permute-done.3 = f32[4,129,128]{2,1,0:T(8,128)S(1)} collective-permute-done((f32[4,129,128]{2,1,0:T(8,128)S(1)}, f32[4,129,128]{2,1,0:T(8,128)S(1)}, u32[]{:S(2)}, u32[]{:S(2)}) %collective-permute-start.3) | collective-permute-done | bytes 264224 | tf_op jit(solution)/shard_map/ppermute | solution.py:38
  108.0 7.4 %collective-permute-done.4 = f32[4,129,128]{2,1,0:T(8,128)S(1)} collective-permute-done((f32[4,129,128]{2,1,0:T(8,128)S(1)}, f32[4,129,128]{2,1,0:T(8,128)S(1)}, u32[]{:S(2)}, u32[]{:S(2)}) %collective-permute-start.4) | collective-permute-done | bytes 264224 | tf_op jit(solution)/shard_map/ppermute | solution.py:38
  117.0 1.8 fusion.7
  118.8 7.1 %collective-permute-done.5 = f32[4,129,128]{2,1,0:T(8,128)} collective-permute-done((f32[4,129,128]{2,1,0:T(8,128)S(1)}, f32[4,129,128]{2,1,0:T(8,128)}, u32[]{:S(2)}, u32[]{:S(2)}) %collective-permute-start.5) | collective-permute-done | bytes 264224 | tf_op jit(solution)/shard_map/ppermute | solution.py:38
  128.6 11.9 %psum.21 = f32[256]{0:T(256)S(1)} all-reduce(f32[256]{0:T(256)S(1)} %get-tuple-element.18), channel_id=1, replica_groups=mesh['seq'=64,'head'=8] {'head'}, use_global_device_ids=true, to_apply=%region_6.7 | all-reduce | flops 256 | bytes 2048 | tf_op jit(solution)/shard_map/psum | solution.py:106
  179.9 62.9 %all_to_all.28 = bf16[64,1,1,10,512]{4,3,2,1,0:T(8,128)(2,1)S(1)} all-to-all(bf16[64,1,1,10,512]{4,3,2,1,0:T(8,128)(2,1)S(1)} %get-tuple-element.22), channel_id=1, replica_groups=mesh['seq'=64,'head'=8] {'seq'}, dimensions={0} | all-to-all | bytes 1310720 | tf_op jit(solution)/shard_map/all_to_all | solution.py:15
  242.9 10.4 %all-to-all-start.2 = ((bf16[64,1,1,10,512]{4,3,2,1,0:T(8,128)(2,1)}), bf16[64,1,1,10,512]{4,3,2,1,0:T(8,128)(2,1)}, u32[]{:S(2)}, u32[]{:S(2)}) async-start(bf16[64,1,1,10,512]{4,3,2,1,0:T(8,128)(2,1)} %get-tuple-element.23), calls=%async_computation.2 | async-start | bytes 2097152 | tf_op jit(solution)/shard_map/all_to_all | solution.py:15
  254.9 3.9 convert_bitcast_fusion
  258.9 81.9 %all-reduce.3.cloned.1.call-done = bf16[1,64,10,2,704]{4,1,3,2,0:T(8,128)(2,1)} async-done(((bf16[1,64,10,2,704]{4,1,3,2,0:T(8,128)(2,1)}), bf16[1,64,10,2,704]{4,1,3,2,0:T(8,128)(2,1)}) %all-reduce.3.cloned.1.call-update) | async-done | bytes 1802256 | tf_op jit(solution)/shard_map/psum | solution.py:145
  340.8 2.0 convert_element_type.115
  346.5 15.5 %all-to-all-start.1 = ((bf16[1,64,10,512]{3,2,0,1:T(8,128)(2,1)}), bf16[1,64,10,512]{3,2,0,1:T(8,128)(2,1)S(1)}, u32[]{:S(2)}, u32[]{:S(2)}) async-start(bf16[1,64,10,512]{3,2,0,1:T(8,128)(2,1)} %bitcast.81), calls=%async_computation.1 | async-start | bytes 2097152 | tf_op jit(solution)/shard_map/all_to_all | solution.py:153
  362.1 3.8 convolution_bitcast_fusion
  365.9 80.3 %all-reduce.5.cloned.1.call-done = bf16[1,64,10,2,704]{4,1,3,2,0:T(8,128)(2,1)} async-done(((bf16[1,64,10,2,704]{4,1,3,2,0:T(8,128)(2,1)}), bf16[1,64,10,2,704]{4,1,3,2,0:T(8,128)(2,1)}) %all-reduce.5.cloned.1.call-update) | async-done | bytes 1802256 | tf_op jit(solution)/shard_map/psum | solution.py:145
  446.3 2.0 convert_element_type.122
  450.8 1.9 convolution_convert_fusion
  453.9 15.5 %all-to-all-start.3 = ((bf16[1,64,10,512]{3,2,0,1:T(8,128)(2,1)}), bf16[1,64,10,512]{3,2,0,1:T(8,128)(2,1)}, u32[]{:S(2)}, u32[]{:S(2)}) async-start(bf16[1,64,10,512]{3,2,0,1:T(8,128)(2,1)} %bitcast.153), calls=%async_computation.3 | async-start | bytes 2097152 | tf_op jit(solution)/shard_map/all_to_all | solution.py:153
  470.2 53.0 %all-to-all-done.3 = bf16[1,64,10,512]{3,2,0,1:T(8,128)(2,1)} async-done(((bf16[1,64,10,512]{3,2,0,1:T(8,128)(2,1)}), bf16[1,64,10,512]{3,2,0,1:T(8,128)(2,1)}, u32[]{:S(2)}, u32[]{:S(2)}) %all-to-all-start.3) | async-done | bytes 655392 | tf_op jit(solution)/shard_map/all_to_all | solution.py:153
  (178 shorter events, 72.0 us)
Async XLA Ops:
  6.5 338.1 %copy-start = (bf16[1,704,512]{2,1,0:T(8,128)(2,1)S(1)}, bf16[1,704,512]{2,1,0:T(8,128)(2,1)}, u32[]{:S(2)}) copy-start(bf16[1,704,512]{2,1,0:T(8,128)(2,1)} %param.21) | copy-start | bytes 2162692
  12.0 17.8 %collective-permute-start = (f32[4,129,128]{2,1,0:T(8,128)S(1)}, f32[4,129,128]{2,1,0:T(8,128)S(1)}, u32[]{:S(2)}, u32[]{:S(2)}) collective-permute-start(f32[4,129,128]{2,1,0:T(8,128)S(1)} %pad_maximum_fusion.1), channel_id=1, source_target_pairs={{0,8},{8,16},{16,24},{24,32},{32,40},{40,48},{48,56},{56,64},{64,7... | collective-permute-start | bytes 792584 | tf_op jit(solution)/shard_map/ppermute | solution.py:38
  30.1 50.0 %copy-start.8 = (s32[256,2]{0,1:T(2,128)S(1)}, s32[256,2]{0,1:T(2,128)}, u32[]{:S(2)}) copy-start(s32[256,2]{0,1:T(2,128)} %param.18) | copy-start | bytes 6148
  30.1 17.9 %collective-permute-start.1 = (f32[4,129,128]{2,1,0:T(8,128)S(1)}, f32[4,129,128]{2,1,0:T(8,128)S(1)}, u32[]{:S(2)}, u32[]{:S(2)}) collective-permute-start(f32[4,129,128]{2,1,0:T(8,128)S(1)} %pad_maximum_fusion.2), channel_id=1, source_target_pairs={{0,16},{8,24},{16,32},{24,40},{32,48},{40,56},{48,64},{56,72},{64,... | collective-permute-start | bytes 792584 | tf_op jit(solution)/shard_map/ppermute | solution.py:38
  48.4 29.5 %collective-permute-start.2 = (f32[4,129,128]{2,1,0:T(8,128)S(1)}, f32[4,129,128]{2,1,0:T(8,128)S(1)}, u32[]{:S(2)}, u32[]{:S(2)}) collective-permute-start(f32[4,129,128]{2,1,0:T(8,128)S(1)} %pad_maximum_fusion.3), channel_id=1, source_target_pairs={{0,32},{8,40},{16,48},{24,56},{32,64},{40,72},{48,80},{56,88},{64,... | collective-permute-start | bytes 792584 | tf_op jit(solution)/shard_map/ppermute | solution.py:38
  78.2 27.2 %collective-permute-start.3 = (f32[4,129,128]{2,1,0:T(8,128)S(1)}, f32[4,129,128]{2,1,0:T(8,128)S(1)}, u32[]{:S(2)}, u32[]{:S(2)}) collective-permute-start(f32[4,129,128]{2,1,0:T(8,128)S(1)} %pad_maximum_fusion.4), channel_id=1, source_target_pairs={{0,64},{8,72},{16,80},{24,88},{32,96},{40,104},{48,112},{56,120},{... | collective-permute-start | bytes 792584 | tf_op jit(solution)/shard_map/ppermute | solution.py:38
  105.8 9.6 %collective-permute-start.4 = (f32[4,129,128]{2,1,0:T(8,128)S(1)}, f32[4,129,128]{2,1,0:T(8,128)S(1)}, u32[]{:S(2)}, u32[]{:S(2)}) collective-permute-start(f32[4,129,128]{2,1,0:T(8,128)S(1)} %pad_maximum_fusion.5), channel_id=1, source_target_pairs={{0,128},{8,136},{16,144},{24,152},{32,160},{40,168},{48,176},{56,1... | collective-permute-start | bytes 792584 | tf_op jit(solution)/shard_map/ppermute | solution.py:38
  115.7 10.3 %collective-permute-start.5 = (f32[4,129,128]{2,1,0:T(8,128)S(1)}, f32[4,129,128]{2,1,0:T(8,128)}, u32[]{:S(2)}, u32[]{:S(2)}) collective-permute-start(f32[4,129,128]{2,1,0:T(8,128)S(1)} %pad_maximum_fusion.6), channel_id=1, source_target_pairs={{0,256},{8,264},{16,272},{24,280},{32,288},{40,296},{48,304},{56,3... | collective-permute-start | bytes 792584 | tf_op jit(solution)/shard_map/ppermute | solution.py:38
  117.0 8.9 %copy-start.6 = (bf16[256,512]{1,0:T(8,128)(2,1)S(1)}, bf16[256,512]{1,0:T(8,128)(2,1)}, u32[]{:S(2)}) copy-start(bf16[256,512]{1,0:T(8,128)(2,1)} %param.12) | copy-start | bytes 786436
  127.4 1.0 copy-start.5
  127.5 0.9 copy-start.9
  127.5 13.0 %copy-start.7 = (pred[640,256]{1,0:T(8,128)(4,1)S(1)}, pred[640,256]{1,0:T(8,128)(4,1)}, u32[]{:S(2)}) copy-start(pred[640,256]{1,0:T(8,128)(4,1)} %fusion.4) | copy-start | bytes 491524
  127.5 13.0 %copy-start.11 = (f32[512]{0:T(512)S(1)}, f32[512]{0:T(512)}, u32[]{:S(2)}) copy-start(f32[512]{0:T(512)} %param.17) | copy-start | bytes 6148
  128.6 11.9 %copy-start.3 = (bf16[256,512]{1,0:T(8,128)(2,1)}, bf16[256,512]{1,0:T(8,128)(2,1)S(1)}, u32[]{:S(2)}) copy-start(bf16[256,512]{1,0:T(8,128)(2,1)S(1)} %get-tuple-element.19) | copy-start | bytes 786436
  242.9 10.4 %copy-start.1 = (bf16[1,512,1408]{2,1,0:T(8,128)(2,1)S(1)}, bf16[1,512,1408]{2,1,0:T(8,128)(2,1)}, u32[]{:S(2)}) copy-start(bf16[1,512,1408]{2,1,0:T(8,128)(2,1)} %param.20) | copy-start | bytes 4325380
  242.9 103.6 %all-to-all-start.2 = ((bf16[64,1,1,10,512]{4,3,2,1,0:T(8,128)(2,1)}), bf16[64,1,1,10,512]{4,3,2,1,0:T(8,128)(2,1)}, u32[]{:S(2)}, u32[]{:S(2)}) async-start(bf16[64,1,1,10,512]{4,3,2,1,0:T(8,128)(2,1)} %get-tuple-element.23), calls=%async_computation.2 | async-start | bytes 2097152 | tf_op jit(solution)/shard_map/all_to_all | solution.py:15
  253.3 87.5 %all-reduce.3.cloned.1.call-start = ((), (), s32[]{:S(2)}) async-start(), calls=%async_computation.4 | async-start | bytes 3932160 | tf_op jit(solution)/shard_map/psum | solution.py:145
  345.3 16.8 %copy-start.2 = (bf16[1,512,1408]{1,2,0:T(8,128)(2,1)S(1)}, bf16[1,512,1408]{1,2,0:T(8,128)(2,1)}, u32[]{:S(2)}) copy-start(bf16[1,512,1408]{1,2,0:T(8,128)(2,1)} %copy.2662) | copy-start | bytes 4325380
  346.5 107.4 %all-to-all-start.1 = ((bf16[1,64,10,512]{3,2,0,1:T(8,128)(2,1)}), bf16[1,64,10,512]{3,2,0,1:T(8,128)(2,1)S(1)}, u32[]{:S(2)}, u32[]{:S(2)}) async-start(bf16[1,64,10,512]{3,2,0,1:T(8,128)(2,1)} %bitcast.81), calls=%async_computation.1 | async-start | bytes 2097152 | tf_op jit(solution)/shard_map/all_to_all | solution.py:153
  362.0 84.2 %all-reduce.5.cloned.1.call-start = ((), (), s32[]{:S(2)}) async-start(), calls=%async_computation.5 | async-start | bytes 3932160 | tf_op jit(solution)/shard_map/psum | solution.py:145
  452.7 16.8 %copy-start.10 = (f32[256,2]{0,1:T(2,128)S(1)}, f32[256,2]{0,1:T(2,128)}, u32[]{:S(2)}) copy-start(f32[256,2]{0,1:T(2,128)} %param.19) | copy-start | bytes 6148
  453.9 69.2 %all-to-all-start.3 = ((bf16[1,64,10,512]{3,2,0,1:T(8,128)(2,1)}), bf16[1,64,10,512]{3,2,0,1:T(8,128)(2,1)}, u32[]{:S(2)}, u32[]{:S(2)}) async-start(bf16[1,64,10,512]{3,2,0,1:T(8,128)(2,1)} %bitcast.153), calls=%async_computation.3 | async-start | bytes 2097152 | tf_op jit(solution)/shard_map/all_to_all | solution.py:153
  529.3 2.0 copy-start.4
Sparse Core Ops, SparseCore 0:
  259.0 81.7 all-reduce.2
  366.1 80.1 all-reduce.4
